TPU v7x, 512 devices: a whole 4x8x8 slice. The times are simulated.
512 devices in a mesh: dp: 16 (over z, core), mp: 32 (over x, y).
Axes of the slice: x: 4, y: 8, z: 8, core: 2. Of those that a mesh axis runs over, the one named last changes fastest.
Arguments:
- tokens: bfloat16 [2048, 4096], P(('dp', 'mp')), may hold values from -6 to 6
- hidden_grad: bfloat16 [2048, 14336], P('dp', 'mp'), may hold values from -0.125 to 0.125
- gate_weight: bfloat16 [4096, 14336], P('dp', 'mp'), may hold values from -0.09375 to 0.09375
- up_weight: bfloat16 [4096, 14336], P('dp', 'mp'), may hold values from -0.09375 to 0.09375
- gate_probe: bfloat16 [4096, 14336], P('dp', 'mp'), may hold values from -1 to 1, as said below
- gate_mean: float32 [4096, 14336], P('dp', 'mp'), may hold values from -0.6 to 0.6
- gate_curve: float32 [4096, 14336], P('dp', 'mp'), may hold values from 1 to 10
- group_counts: int32 [16], replicated, may hold values from 32 to 128, as said below
Outputs:
- gate_weight_new: bfloat16 [4096, 14336], P('dp', 'mp')
- gate_mean_new: float32 [4096, 14336], P('dp', 'mp')
- gate_curve_new: float32 [4096, 14336], P('dp', 'mp')
Inputs may be any that keep to these rules, and one draw needn't show every extreme that they name: `group_counts`: some data group has exactly 128 live tokens in every draw. `gate_probe`: every entry is -1 or 1, each sign drawn independently.
All inputs are finite; a program needn't handle non-finite values.
Results may differ from a plain program's by a relative error of at most 0.0017.
Values may be sent and summed in bfloat16 or wider, within the bound.
No kernel may reach another device: no remote copies, remote signals or barrier semaphores. Data moves between devices by JAX's collectives and lax.ppermute only.
A program may use at most 64 MiB of HBM per device.

v0:
```python
import jax
import jax.numpy as jnp
from jax import lax
from jax.sharding import PartitionSpec as P

first_decay = 0.9
second_decay = 0.999
learn_rate = 0.15
epsilon_term = 0.0001
first_fix = 1.0 - 0.9**10
second_fix = 1.0 - 0.999**10


def silu_parts(inputs):
    sigmoid_part = jax.nn.sigmoid(inputs)
    silu_slope = sigmoid_part * (1.0 + inputs * (1.0 - sigmoid_part))
    silu_bend = sigmoid_part * (1.0 - sigmoid_part) * (2.0 + inputs * (1.0 - 2.0 * sigmoid_part))
    return (silu_slope, silu_bend)


def adahessian(weight, mean_old, curve_old, gradient, probe_value, product):
    diagonal = probe_value.astype(jnp.float32) * product
    mean_new = first_decay * mean_old + (1.0 - first_decay) * gradient
    curve_new = second_decay * curve_old + (1.0 - second_decay) * diagonal * diagonal
    step_ratio = mean_new / first_fix / (jnp.sqrt(curve_new / second_fix) + epsilon_term)
    weight_new = (weight.astype(jnp.float32) - learn_rate * step_ratio).astype(jnp.bfloat16)
    return (weight_new, mean_new, curve_new)


def body(
    tokens, hidden_grad, gate_weight, up_weight, gate_probe, gate_mean, gate_curve, group_counts
):
    whole = lax.all_gather(tokens, "mp", axis=0, tiled=True)
    columns = lax.all_to_all(whole, "dp", split_axis=1, concat_axis=0, tiled=True)
    group_rows = whole.shape[0]
    width = gate_weight.shape[1]
    pieces = (
        lax.all_gather(gate_weight, "dp", axis=0, tiled=True),
        lax.all_gather(up_weight, "dp", axis=0, tiled=True),
    )
    gate_pre, up_pre = tuple(
        (jnp.dot(whole, piece, preferred_element_type=jnp.float32) for piece in pieces)
    )
    selected = columns
    gate_tan = lax.psum_scatter(
        jnp.dot(selected, gate_probe, preferred_element_type=jnp.float32),
        "dp",
        scatter_dimension=0,
        tiled=True,
    )
    group_index = lax.axis_index("dp")
    limit = lax.dynamic_index_in_dim(group_counts, group_index, 0, keepdims=False)
    live = (jnp.arange(group_rows, dtype=jnp.int32) < limit).astype(jnp.float32)
    silu_slope, silu_bend = silu_parts(gate_pre)
    masked = hidden_grad.astype(jnp.float32) * live[:, None]
    grad_gate = (masked * up_pre * silu_slope).astype(jnp.bfloat16)
    tan_gate = (masked * up_pre * silu_bend * gate_tan).astype(jnp.bfloat16)
    packed = jnp.concatenate([grad_gate, tan_gate], 1)
    selected = columns
    sums = lax.dot_general(
        selected,
        lax.all_gather(packed, "dp", axis=0, tiled=True),
        (((0,), (0,)), ((), ())),
        preferred_element_type=jnp.float32,
    )
    gate_out = adahessian(
        gate_weight, gate_mean, gate_curve, sums[:, :width], gate_probe, sums[:, width:]
    )
    return (gate_out[0], gate_out[1], gate_out[2])


def solution(mesh):
    return jax.shard_map(
        body,
        mesh=mesh,
        in_specs=(
            P(("dp", "mp"), None),
            P("dp", "mp"),
            P("dp", "mp"),
            P("dp", "mp"),
            P("dp", "mp"),
            P("dp", "mp"),
            P("dp", "mp"),
            P(),
        ),
        out_specs=(P("dp", "mp"), P("dp", "mp"), P("dp", "mp")),
        check_vma=False,
    )
```

profile of v0, /device:TPU:1, one launch (start us, length us, event | category | flops | bytes accessed | tf_op | source)
XLA Modules:
  0.0 342.0 jit_solution(2087898380235495970)
XLA Ops:
  7.2 0.0 all-gather.12.cloned.1.call-start
  7.2 0.7 all-gather.12.cloned.1.call-update
  7.9 0.0 all-gather.8.cloned.1.call-start
  8.0 0.7 all-gather.8.cloned.1.call-update
  8.7 0.0 all-gather.6.cloned.1.call-start
  8.7 0.7 all-gather.6.cloned.1.call-update
  9.4 0.0 reduce-scatter.2.cloned.1.call-start
  9.4 83.9 %all-gather.12.cloned.1.call-done = bf16[32,4,4096]{2,1,0:T(4,128)(2,1)} async-done(((bf16[1,4,4096]{2,1,0:T(4,128)(2,1)}), bf16[32,4,4096]{2,1,0:T(4,128)(2,1)}) %all-gather.12.cloned.1.call-update) | async-done | bytes 1048592 | tf_op jit(solution)/shard_map/all_gather | solution.py:33
  93.3 1.8 all_to_all.14
  95.1 0.3 copy.12
  95.5 47.8 %all_to_all.19 = bf16[128,16,256]{2,0,1:T(8,128)(2,1)S(1)} all-to-all(bf16[128,16,256]{2,0,1:T(8,128)(2,1)S(1)} %copy.12), channel_id=1, replica_groups=mesh['dp'=16,'mp'=32] {'dp'}, dimensions={1} | all-to-all | bytes 2097152 | tf_op jit(solution)/shard_map/all_to_all | solution.py:34
  143.3 2.6 fusion.13
  145.9 0.0 reduce-scatter.2.cloned.1.call-update
  145.9 0.0 copy-start.5
  145.9 0.0 all-gather.10.cloned.1.call-start
  146.0 0.6 copy-done.6
  146.5 0.6 dynamic_slice.4
  147.1 0.6 compare_convert_fusion
  147.8 0.3 reshape.15
  148.1 15.2 %all-gather.8.cloned.1.call-done = bf16[4096,448]{0,1:T(8,128)(2,1)} async-done(((bf16[256,448]{0,1:T(8,128)(2,1)}), bf16[4096,448]{0,1:T(8,128)(2,1)}) %all-gather.8.cloned.1.call-update) | async-done | bytes 3670032 | tf_op jit(solution)/shard_map/all_gather | solution.py:38
  163.3 3.1 fusion.12
  166.5 45.4 %all-gather.6.cloned.1.call-done = bf16[4096,448]{0,1:T(8,128)(2,1)} async-done(((bf16[256,448]{0,1:T(8,128)(2,1)}), bf16[4096,448]{0,1:T(8,128)(2,1)}) %all-gather.6.cloned.1.call-update) | async-done | bytes 3670032 | tf_op jit(solution)/shard_map/all_gather | solution.py:39
  211.9 63.9 %reduce-scatter.2.cloned.1.call-done = f32[128,448]{0,1:T(8,128)} async-done(((f32[2048,448]{0,1:T(8,128)}), f32[128,448]{0,1:T(8,128)}) %reduce-scatter.2.cloned.1.call-update) | async-done | bytes 229392 | tf_op jit(solution)/shard_map/reduce_scatter | solution.py:45
  275.8 3.2 fusion.5
  278.9 0.7 pad_maximum_fusion
  279.6 0.0 all-gather.10.cloned.1.call-update
  279.7 0.0 copy-start.1
  279.7 0.0 copy-start.3
  279.7 0.0 copy-start.4
  279.7 51.3 %all-gather.10.cloned.1.call-done = bf16[2048,896]{0,1:T(8,128)(2,1)} async-done(((bf16[128,896]{0,1:T(8,128)(2,1)}), bf16[2048,896]{0,1:T(8,128)(2,1)}) %all-gather.10.cloned.1.call-update) | async-done | bytes 3670032 | tf_op jit(solution)/shard_map/all_gather | solution.py:62
  331.0 3.1 convolution_bitcast_fusion
  334.2 1.2 subtract_convert_fusion
  (9 shorter events, 0.0 us)
Async XLA Ops:
  7.2 136.1 %copy-start.2 = (bf16[256,448]{0,1:T(8,128)(2,1)S(1)}, bf16[256,448]{0,1:T(8,128)(2,1)}, u32[]{:S(2)}) copy-start(bf16[256,448]{0,1:T(8,128)(2,1)} %param.12) | copy-start | bytes 688132
  7.2 86.2 %all-gather.12.cloned.1.call-start = ((), (), s32[]{:S(2)}) async-start(), calls=%async_computation.6 | async-start | bytes 1081344 | tf_op jit(solution)/shard_map/all_gather | solution.py:33
  7.9 155.4 %all-gather.8.cloned.1.call-start = ((), (), s32[]{:S(2)}) async-start(), calls=%async_computation.3 | async-start | bytes 3899392 | tf_op jit(solution)/shard_map/all_gather | solution.py:38
  8.7 203.2 %all-gather.6.cloned.1.call-start = ((), (), s32[]{:S(2)}) async-start(), calls=%async_computation.2 | async-start | bytes 3899392 | tf_op jit(solution)/shard_map/all_gather | solution.py:39
  9.4 266.4 %reduce-scatter.2.cloned.1.call-start = ((), (), s32[]{:S(2)}) async-start(), calls=%async_computation.4 | async-start | bytes 3899392 | tf_op jit(solution)/shard_map/reduce_scatter | solution.py:45
  145.9 0.7 copy-start.6
  145.9 1.9 copy-start
  145.9 129.9 %copy-start.5 = (bf16[128,448]{0,1:T(8,128)(2,1)S(1)}, bf16[128,448]{0,1:T(8,128)(2,1)}, u32[]{:S(2)}) copy-start(bf16[128,448]{0,1:T(8,128)(2,1)} %param.9) | copy-start | bytes 344068
  145.9 185.1 %all-gather.10.cloned.1.call-start = ((), (), s32[]{:S(2)}) async-start(), calls=%async_computation.5 | async-start | bytes 3899392 | tf_op jit(solution)/shard_map/all_gather | solution.py:62
  279.7 54.5 %copy-start.1 = (bf16[256,448]{0,1:T(8,128)(2,1)S(1)}, bf16[256,448]{0,1:T(8,128)(2,1)}, u32[]{:S(2)}) copy-start(bf16[256,448]{0,1:T(8,128)(2,1)} %param.10) | copy-start | bytes 688132
  279.7 54.5 %copy-start.3 = (f32[256,448]{0,1:T(8,128)S(1)}, f32[256,448]{0,1:T(8,128)}, u32[]{:S(2)}) copy-start(f32[256,448]{0,1:T(8,128)} %param.13) | copy-start | bytes 1376260
  279.7 54.5 %copy-start.4 = (f32[256,448]{0,1:T(8,128)S(1)}, f32[256,448]{0,1:T(8,128)}, u32[]{:S(2)}) copy-start(f32[256,448]{0,1:T(8,128)} %param.14) | copy-start | bytes 1376260
Sparse Core Ops, SparseCore 0:
  11.2 82.1 all-gather.11
  95.4 67.8 all-gather.7
  165.4 46.4 all-gather.5
  214.6 61.1 reduce-scatter.1
  279.8 51.2 all-gather.9
where the time goes:
time: 342 us
  waiting for transfers between devices  262 us (77%)
  blocking collectives  47.8 us (14%)
  between operations  13.9 us (4%)
  matrix products  12 us (4%)
  local copies, waits for them, and re-layouts  3.58 us (1%)
    all_gather x1, waiting for transfers between devices, body(): whole = lax.all_gather(tokens, 'mp', axis=0, tiled=True)  83.9 us
    reduce_scatter x1, waiting for transfers between devices, body(): lax.psum_scatter(jnp.dot(selected, gate_probe, preferred_element_type=jnp...  63.9 us
    all_gather x1, waiting for transfers between devices, body(): lax.all_gather(packed, 'dp', axis=0, tiled=True)  51.3 us
    all_to_all x1, blocking collectives, body(): lax.all_to_all(whole, 'dp', split_axis=1, concat_axis=0, tiled=True)  47.8 us
    all_gather x1, waiting for transfers between devices, body(): lax.all_gather(up_weight, 'dp', axis=0, tiled=True)  45.4 us
    all_gather x1, waiting for transfers between devices, body(): lax.all_gather(gate_weight, 'dp', axis=0, tiled=True)  15.2 us
  transfers between devices with their start and end apart: 5, of which 5 were waited for; matrix products, arithmetic and copies ran while one was open for 2% of the time, Pallas kernels for 0%

commit v1 on v0

--- a/solution.py
+++ b/solution.py
@@ -30,7 +30,8 @@
 def body(
     tokens, hidden_grad, gate_weight, up_weight, gate_probe, gate_mean, gate_curve, group_counts
 ):
-    whole = lax.all_gather(tokens, "mp", axis=0, tiled=True)
+    stack = jnp.stack([tokens] * lax.axis_size("mp"))
+    whole = jnp.concatenate(lax.all_to_all(stack, "mp", 0, 0), axis=0)
     columns = lax.all_to_all(whole, "dp", split_axis=1, concat_axis=0, tiled=True)
     group_rows = whole.shape[0]
     width = gate_weight.shape[1]

time: 342 us -> 259 us (0.76)
  waiting for transfers between devices: 262 us -> 148 us
  blocking collectives: 47.8 us -> 78.3 us
    all_gather x1 -> x0, waiting for transfers between devices: 83.9 us -> none  [body(): whole = lax.all_gather(tokens, 'mp', axis=0, tiled=True)]
    all_to_all x0 -> x1, blocking collectives: none -> 35.2 us  [body(): whole = jnp.concatenate(lax.all_to_all(stack, 'mp', 0, 0), axis=0)]
    all_gather x1, waiting for transfers between devices: 15.2 us -> 0.02 us  [body(): lax.all_gather(gate_weight, 'dp', axis=0, tiled=True)]
    all_gather x1, waiting for transfers between devices: 45.4 us -> 31 us  [body(): lax.all_gather(up_weight, 'dp', axis=0, tiled=True)]
    all_to_all x1, blocking collectives: 47.8 us -> 43.2 us  [body(): lax.all_to_all(whole, 'dp', split_axis=1, concat_axis=0, tiled=True)]
  transfers between devices with their start and end apart: 5 -> 4, of which waited for: 5 -> 3; matrix products, arithmetic and copies ran while one was open for 2% -> 3% of each run, Pallas kernels for 0% -> 0%
where the time goes in v1:
time: 259 us
  waiting for transfers between devices  148 us (57%)
  blocking collectives  78.3 us (30%)
  between operations  13.9 us (5%)
  matrix products  12 us (5%)
  local copies, waits for them, and re-layouts  3.77 us (1%)
  other arithmetic  2.59 us (1%)
    reduce_scatter x1, waiting for transfers between devices, body(): lax.psum_scatter(jnp.dot(selected, gate_probe, preferred_element_type=jnp...  64.1 us
    all_gather x1, waiting for transfers between devices, body(): lax.all_gather(packed, 'dp', axis=0, tiled=True)  51.3 us
    all_to_all x1, blocking collectives, body(): lax.all_to_all(whole, 'dp', split_axis=1, concat_axis=0, tiled=True)  43.2 us
    all_to_all x1, blocking collectives, body(): whole = jnp.concatenate(lax.all_to_all(stack, 'mp', 0, 0), axis=0)  35.2 us
    all_gather x1, waiting for transfers between devices, body(): lax.all_gather(up_weight, 'dp', axis=0, tiled=True)  31 us
    dot_general x2, matrix products, body(): jnp.dot(whole, piece, preferred_element_type=jnp.float32)  6.31 us
  transfers between devices with their start and end apart: 4, of which 3 were waited for; matrix products, arithmetic and copies ran while one was open for 3% of the time, Pallas kernels for 0%

profile of v1, /device:TPU:1, one launch (start us, length us, event | category | flops | bytes accessed | tf_op | source)
XLA Modules:
  0.0 258.6 jit_solution(155342898958933534)
XLA Ops:
  7.2 0.0 all-gather.6.cloned.1.call-start
  7.2 0.7 all-gather.6.cloned.1.call-update
  7.9 0.0 all-gather.4.cloned.1.call-start
  7.9 0.7 all-gather.4.cloned.1.call-update
  8.6 0.0 reduce-scatter.2.cloned.1.call-start
  8.7 1.2 stack.2
  9.9 35.2 %all_to_all.24 = bf16[32,4,4096]{2,1,0:T(4,128)(2,1)S(1)} all-to-all(bf16[32,4,4096]{2,1,0:T(4,128)(2,1)S(1)} %stack.2), channel_id=1, replica_groups=mesh['dp'=16,'mp'=32] {'mp'}, dimensions={0} | all-to-all | bytes 2097152 | tf_op jit(solution)/shard_map/all_to_all | solution.py:34
  45.1 0.8 all_to_all.18
  45.8 0.3 copy.12
  46.2 43.2 %all_to_all.25 = bf16[128,16,256]{2,0,1:T(8,128)(2,1)S(1)} all-to-all(bf16[128,16,256]{2,0,1:T(8,128)(2,1)S(1)} %copy.12), channel_id=1, replica_groups=mesh['dp'=16,'mp'=32] {'dp'}, dimensions={1} | all-to-all | bytes 2097152 | tf_op jit(solution)/shard_map/all_to_all | solution.py:35
  89.4 0.0 copy-done.1
  89.4 2.6 fusion.13
  91.9 0.0 reduce-scatter.2.cloned.1.call-update
  92.0 0.0 copy-start.4
  92.0 0.0 all-gather.8.cloned.1.call-start
  92.0 0.6 copy-done.5
  92.6 0.6 dynamic_slice.4
  93.2 0.6 compare_convert_fusion
  93.8 0.3 reshape.20
  94.1 0.0 all-gather.6.cloned.1.call-done
  94.2 3.1 %fusion.12 = f32[128,448]{0,1:T(8,128)S(1)} fusion(bf16[128,4096]{1,0:T(8,128)(2,1)S(1)} %reshape.20, bf16[4096,448]{0,1:T(8,128)(2,1)} %all-gather.6.cloned.1.call-done), kind=kOutput, calls=%fused_computation.21 | convolution fusion | flops 469762048 | bytes 4947968 | tf_op jit(solution)/shard_map/dot_general | solution.py:43
  97.3 31.0 %all-gather.4.cloned.1.call-done = bf16[4096,448]{0,1:T(8,128)(2,1)} async-done(((bf16[256,448]{0,1:T(8,128)(2,1)}), bf16[4096,448]{0,1:T(8,128)(2,1)}) %all-gather.4.cloned.1.call-update) | async-done | bytes 3670032 | tf_op jit(solution)/shard_map/all_gather | solution.py:40
  128.3 64.1 %reduce-scatter.2.cloned.1.call-done = f32[128,448]{0,1:T(8,128)} async-done(((f32[2048,448]{0,1:T(8,128)}), f32[128,448]{0,1:T(8,128)}) %reduce-scatter.2.cloned.1.call-update) | async-done | bytes 229392 | tf_op jit(solution)/shard_map/reduce_scatter | solution.py:46
  192.4 3.2 %fusion.5 = (bf16[128,448]{0,1:T(8,128)(2,1)S(1)}, bf16[128,448]{0,1:T(8,128)(2,1)S(1)}) fusion(f32[128,448]{0,1:T(8,128)S(1)} %fusion.12, f32[128,448]{0,1:T(8,128)} %reduce-scatter.2.cloned.1.call-done, bf16[128,4096]{1,0:T(8,128)(2,1)S(1)} %reshape.20, bf16[4096,448]{0,1:T(8,128)(2,1)} %all-gather.4.cloned.1.call-done, f32[128]{0:T(128)S(1)} %compare_convert_fusion, ...), kind=kOutput, calls=%fused_computation.13 | convolution fusion | flops 470966272 | bytes 5521920 | tf_op jit(solution)/shard_map/dot_general | solution.py:43
  195.6 0.7 pad_maximum_fusion
  196.3 0.0 all-gather.8.cloned.1.call-update
  196.3 0.0 copy-start
  196.3 0.0 copy-start.2
  196.3 0.0 copy-start.3
  196.3 51.3 %all-gather.8.cloned.1.call-done = bf16[2048,896]{0,1:T(8,128)(2,1)} async-done(((bf16[128,896]{0,1:T(8,128)(2,1)}), bf16[2048,896]{0,1:T(8,128)(2,1)}) %all-gather.8.cloned.1.call-update) | async-done | bytes 3670032 | tf_op jit(solution)/shard_map/all_gather | solution.py:63
  247.7 3.1 %convolution_bitcast_fusion = f32[256,896]{0,1:T(8,128)S(1)} fusion(bf16[2048,896]{0,1:T(8,128)(2,1)} %all-gather.8.cloned.1.call-done, bf16[2048,256]{1,0:T(8,128)(2,1)S(1)} %bitcast.15), kind=kOutput, calls=%fused_computation | convolution fusion | flops 939524096 | bytes 5636096 | tf_op jit(solution)/shard_map/dot_general | solution.py:61
  250.9 1.2 subtract_convert_fusion
  (6 shorter events, 0.0 us)
Async XLA Ops:
  7.2 87.0 %all-gather.6.cloned.1.call-start = ((), (), s32[]{:S(2)}) async-start(), calls=%async_computation.4 | async-start | bytes 3899392 | tf_op jit(solution)/shard_map/all_gather | solution.py:39
  7.9 120.4 %all-gather.4.cloned.1.call-start = ((), (), s32[]{:S(2)}) async-start(), calls=%async_computation.3 | async-start | bytes 3899392 | tf_op jit(solution)/shard_map/all_gather | solution.py:40
  8.6 183.8 %reduce-scatter.2.cloned.1.call-start = ((), (), s32[]{:S(2)}) async-start(), calls=%async_computation.5 | async-start | bytes 3899392 | tf_op jit(solution)/shard_map/reduce_scatter | solution.py:46
  45.1 44.3 %copy-start.1 = (bf16[256,448]{0,1:T(8,128)(2,1)S(1)}, bf16[256,448]{0,1:T(8,128)(2,1)}, u32[]{:S(2)}) copy-start(bf16[256,448]{0,1:T(8,128)(2,1)} %param.12) | copy-start | bytes 688132
  91.9 0.7 copy-start.5
  92.0 100.4 %copy-start.4 = (bf16[128,448]{0,1:T(8,128)(2,1)S(1)}, bf16[128,448]{0,1:T(8,128)(2,1)}, u32[]{:S(2)}) copy-start(bf16[128,448]{0,1:T(8,128)(2,1)} %param.9) | copy-start | bytes 344068
  92.0 155.7 %all-gather.8.cloned.1.call-start = ((), (), s32[]{:S(2)}) async-start(), calls=%async_computation.6 | async-start | bytes 3899392 | tf_op jit(solution)/shard_map/all_gather | solution.py:63
  196.3 54.5 %copy-start = (bf16[256,448]{0,1:T(8,128)(2,1)S(1)}, bf16[256,448]{0,1:T(8,128)(2,1)}, u32[]{:S(2)}) copy-start(bf16[256,448]{0,1:T(8,128)(2,1)} %param.10) | copy-start | bytes 688132
  196.3 54.5 %copy-start.2 = (f32[256,448]{0,1:T(8,128)S(1)}, f32[256,448]{0,1:T(8,128)}, u32[]{:S(2)}) copy-start(f32[256,448]{0,1:T(8,128)} %param.13) | copy-start | bytes 1376260
  196.3 54.5 %copy-start.3 = (f32[256,448]{0,1:T(8,128)S(1)}, f32[256,448]{0,1:T(8,128)}, u32[]{:S(2)}) copy-start(f32[256,448]{0,1:T(8,128)} %param.14) | copy-start | bytes 1376260
Sparse Core Ops, SparseCore 0:
  10.0 56.0 all-gather.5
  68.2 60.1 all-gather.3
  131.2 61.1 reduce-scatter.1
  196.4 51.1 all-gather.7
